TPU v7x, 128 devices: a whole 4x4x4 slice. The times are simulated.
128 devices in a mesh: grp: 8 (over z, core), dev: 16 (over y, x).
Axes of the slice: x: 4, y: 4, z: 4, core: 2. Of those that a mesh axis runs over, the one named last changes fastest.
Arguments:
- positions: float32 [3, 131072], P(None, ('grp', 'dev')), may hold values from -3 to 3
- velocities: float32 [3, 131072], P(None, ('grp', 'dev')), may hold values from -5 to 5
- accelerations: float32 [3, 131072], P(None, ('grp', 'dev')), may hold values from -3 to 3
- jerks: float32 [3, 131072], P(None, ('grp', 'dev')), may hold values from -3 to 3
- levels: int32 [131072], P(('grp', 'dev')), may hold values from 0 to 5
- counts: int32 [2, 128], replicated, may hold values from 1 to 256, 16384 in all within a row
- active_rows: int32 [2, 32768], P(None, ('grp', 'dev')), may hold values from 0 to 1023, as said below
Outputs:
- new_positions: float32 [3, 131072], P(None, ('grp', 'dev'))
- new_velocities: float32 [3, 131072], P(None, ('grp', 'dev'))
- new_accelerations: float32 [3, 131072], P(None, ('grp', 'dev'))
- new_jerks: float32 [3, 131072], P(None, ('grp', 'dev'))
Inputs may be any that keep to these rules, and one draw needn't show every extreme that they name: In each step the 128 counts sum to exactly 16384 and the largest of them is exactly 256. `active_rows`: for each step and device, the 256 entries of the device's slots are distinct indices of that device's own stars; only the first counts of them are live.
All inputs are finite; a program needn't handle non-finite values.
Results may differ from a plain program's by a relative error of at most 0.00022.
Values sent between devices are 32-bit elements; how exact they have to be, the bound alone decides.
No kernel may reach another device: no remote copies, remote signals or barrier semaphores. Data moves between devices by JAX's collectives and lax.ppermute only.
A program may use at most 128 MiB of HBM per device.

v0:
```python
import math
import jax
import jax.numpy as jnp
from jax import lax
from jax.sharding import PartitionSpec as P

tick_length = 1.0 / 128.0


def pair_block(targets, src_pos, src_vel, mass, soft_sq):
    gap_x = src_pos[0][None, :] - targets[0][:, None]
    gap_y = src_pos[1][None, :] - targets[1][:, None]
    gap_z = src_pos[2][None, :] - targets[2][:, None]
    drift_x = src_vel[0][None, :] - targets[3][:, None]
    drift_y = src_vel[1][None, :] - targets[4][:, None]
    drift_z = src_vel[2][None, :] - targets[5][:, None]
    squared = gap_x * gap_x + gap_y * gap_y + gap_z * gap_z + soft_sq
    inverse = lax.rsqrt(squared)
    weight = mass * inverse * inverse * inverse
    along = 3.0 * (gap_x * drift_x + gap_y * drift_y + gap_z * drift_z) * inverse * inverse
    return jnp.stack(
        [
            jnp.sum(weight * gap_x, axis=1),
            jnp.sum(weight * gap_y, axis=1),
            jnp.sum(weight * gap_z, axis=1),
            jnp.sum(weight * (drift_x - along * gap_x), axis=1),
            jnp.sum(weight * (drift_y - along * gap_y), axis=1),
            jnp.sum(weight * (drift_z - along * gap_z), axis=1),
        ]
    )


def block_terms(packed, src_pos, src_vel, mass, soft_sq):
    width, total = packed.shape
    block = math.gcd(total, 2048)
    grouped = packed.reshape(width, total // block, block).transpose(1, 0, 2)
    result = lax.map(lambda targets: pair_block(targets, src_pos, src_vel, mass, soft_sq), grouped)
    return result.transpose(1, 0, 2).reshape(width, total)


def predict(positions, velocities, accelerations, jerks, elapsed):
    span = elapsed[None, :]
    pred_pos = (
        positions
        + span * velocities
        + 0.5 * span * span * accelerations
        + span * span * span / 6.0 * jerks
    )
    pred_vel = velocities + span * accelerations + 0.5 * span * span * jerks
    return (pred_pos, pred_vel)


def correct(old_pos, old_vel, old_acc, old_jerk, force, jerk_new, span):
    span = span[None, :]
    new_vel = old_vel + 0.5 * span * (old_acc + force) + span * span / 12.0 * (old_jerk - jerk_new)
    new_pos = old_pos + 0.5 * span * (old_vel + new_vel) + span * span / 12.0 * (old_acc - force)
    return (new_pos, new_vel)


def shards(positions, velocities, accelerations, jerks, levels, counts, active_rows):
    devices_all = lax.axis_size("grp") * lax.axis_size("dev")
    my_rank = lax.axis_index("grp") * lax.axis_size("dev") + lax.axis_index("dev")
    star_dev = positions.shape[1]
    slot_cap = active_rows.shape[1]
    stars_all = star_dev * devices_all
    mass = 1.0 / stars_all
    soft_sq = 0.0004 * (131072.0 / stars_all) ** (2.0 / 3.0)
    last_time = -(jnp.left_shift(jnp.int32(1), levels) - 1).astype(jnp.float32) * tick_length
    for step in range(active_rows.shape[0]):
        now = (step + 1) * tick_length
        pred_pos, pred_vel = predict(positions, velocities, accelerations, jerks, now - last_time)
        rows = active_rows[step]
        targets = jnp.concatenate([pred_pos[:, rows], pred_vel[:, rows]], axis=0)
        step_counts = counts[step]
        own_count = step_counts[my_rank]
        gathered = lax.all_gather(targets[None], ("grp", "dev"), axis=0, tiled=True)
        flat = gathered.transpose(1, 0, 2).reshape(6, devices_all * slot_cap)
        terms = block_terms(flat, pred_pos, pred_vel, mass, soft_sq)
        totals = lax.psum(terms, ("grp", "dev"))
        own = lax.dynamic_slice_in_dim(totals, my_rank * slot_cap, slot_cap, 1)
        span = now - last_time[rows]
        new_pos, new_vel = correct(
            positions[:, rows],
            velocities[:, rows],
            accelerations[:, rows],
            jerks[:, rows],
            own[:3],
            own[3:],
            span,
        )
        live = jnp.arange(slot_cap, dtype=jnp.int32) < own_count
        target = jnp.where(live, rows, star_dev)
        positions = positions.at[:, target].set(new_pos, mode="drop")
        velocities = velocities.at[:, target].set(new_vel, mode="drop")
        accelerations = accelerations.at[:, target].set(own[:3], mode="drop")
        jerks = jerks.at[:, target].set(own[3:], mode="drop")
        last_time = last_time.at[target].set(now, mode="drop")
    return (positions, velocities, accelerations, jerks)


def solution(mesh):
    placed = (
        P(None, ("grp", "dev")),
        P(None, ("grp", "dev")),
        P(None, ("grp", "dev")),
        P(None, ("grp", "dev")),
        P(("grp", "dev")),
        P(),
        P(None, ("grp", "dev")),
    )
    return jax.shard_map(
        shards,
        mesh=mesh,
        in_specs=placed,
        out_specs=(
            P(None, ("grp", "dev")),
            P(None, ("grp", "dev")),
            P(None, ("grp", "dev")),
            P(None, ("grp", "dev")),
        ),
        check_vma=False,
    )
```

profile of v0, /device:TPU:1, one launch (start us, length us, event | category | flops | bytes accessed | tf_op | source)
XLA Modules:
  0.0 1007.9 jit_solution(7098034643428185469)
XLA Ops:
  14.2 63.9 %all-gather.2 = f32[128,6,256]{2,1,0:T(8,128)S(1)} all-gather(f32[1,6,256]{2,1,0:T(8,128)S(1)} %maximum_bitcast_fusion), channel_id=2, replica_groups=mesh['grp'=8,'dev'=16] {'grp','dev'}, dimensions={0}, use_global_device_ids=true | all-gather | bytes 792576 | tf_op jit(solution)/shard_map/all_gather | solution.py:76
  78.2 263.2 %while.20 = (s32[]{:T(128)}, f32[16,6,2048]{2,1,0:T(8,128)S(1)}, f32[3,1024]{1,0:T(4,128)S(1)}, f32[16,6,2048]{2,1,0:T(8,128)S(1)}, f32[3,1024]{1,0:T(4,128)S(1)...) while((s32[]{:T(128)}, f32[16,6,2048]{2,1,0:T(8,128)S(1)}, ...), condition=%wide.region_7.8_spmd, body=%wide.region_0.7_spmd.sunk | while | flops 85970952 | bytes 499917 | solution.py:37
  78.3 16.2 %fusion.64 = (f32[2048]{0:T(1024)S(1)}, f32[2048]{0:T(1024)S(1)}, f32[2048]{0:T(1024)S(1)}, f32[2048]{0:T(1024)S(1)}, f32[2048]{0:T(1024)S(1)}, /*index=5*/f32[2048]{0:T(1024)S(1)}) fusion(f32[2048]{0:T(1024)S(1)} %bitcast.257, f32[1024]{0:T(1024)S(1)} %bitcast.269, f32[2048]{0:T(1024)S(1)} %bitcast.254, f32[1024]{0:T(1024)S(1)} %bitcast.272, ...), kind=kLoop, calls=%fused_computation.45.clone.1 | loop fusion | flops 85970944 | bytes 122880 | tf_op jit(solution)/shard_map/while/body/eval_jaxpr/reduce_sum | solution.py:28
  94.8 16.2 %fusion.64 = (f32[2048]{0:T(1024)S(1)}, f32[2048]{0:T(1024)S(1)}, f32[2048]{0:T(1024)S(1)}, f32[2048]{0:T(1024)S(1)}, f32[2048]{0:T(1024)S(1)}, /*index=5*/f32[2048]{0:T(1024)S(1)}) fusion(f32[2048]{0:T(1024)S(1)} %bitcast.257, f32[1024]{0:T(1024)S(1)} %bitcast.269, f32[2048]{0:T(1024)S(1)} %bitcast.254, f32[1024]{0:T(1024)S(1)} %bitcast.272, ...), kind=kLoop, calls=%fused_computation.45.clone.1 | loop fusion | flops 85970944 | bytes 122880 | tf_op jit(solution)/shard_map/while/body/eval_jaxpr/reduce_sum | solution.py:28
  111.2 16.2 %fusion.64 = (f32[2048]{0:T(1024)S(1)}, f32[2048]{0:T(1024)S(1)}, f32[2048]{0:T(1024)S(1)}, f32[2048]{0:T(1024)S(1)}, f32[2048]{0:T(1024)S(1)}, /*index=5*/f32[2048]{0:T(1024)S(1)}) fusion(f32[2048]{0:T(1024)S(1)} %bitcast.257, f32[1024]{0:T(1024)S(1)} %bitcast.269, f32[2048]{0:T(1024)S(1)} %bitcast.254, f32[1024]{0:T(1024)S(1)} %bitcast.272, ...), kind=kLoop, calls=%fused_computation.45.clone.1 | loop fusion | flops 85970944 | bytes 122880 | tf_op jit(solution)/shard_map/while/body/eval_jaxpr/reduce_sum | solution.py:28
  127.7 16.2 %fusion.64 = (f32[2048]{0:T(1024)S(1)}, f32[2048]{0:T(1024)S(1)}, f32[2048]{0:T(1024)S(1)}, f32[2048]{0:T(1024)S(1)}, f32[2048]{0:T(1024)S(1)}, /*index=5*/f32[2048]{0:T(1024)S(1)}) fusion(f32[2048]{0:T(1024)S(1)} %bitcast.257, f32[1024]{0:T(1024)S(1)} %bitcast.269, f32[2048]{0:T(1024)S(1)} %bitcast.254, f32[1024]{0:T(1024)S(1)} %bitcast.272, ...), kind=kLoop, calls=%fused_computation.45.clone.1 | loop fusion | flops 85970944 | bytes 122880 | tf_op jit(solution)/shard_map/while/body/eval_jaxpr/reduce_sum | solution.py:28
  144.2 16.2 %fusion.64 = (f32[2048]{0:T(1024)S(1)}, f32[2048]{0:T(1024)S(1)}, f32[2048]{0:T(1024)S(1)}, f32[2048]{0:T(1024)S(1)}, f32[2048]{0:T(1024)S(1)}, /*index=5*/f32[2048]{0:T(1024)S(1)}) fusion(f32[2048]{0:T(1024)S(1)} %bitcast.257, f32[1024]{0:T(1024)S(1)} %bitcast.269, f32[2048]{0:T(1024)S(1)} %bitcast.254, f32[1024]{0:T(1024)S(1)} %bitcast.272, ...), kind=kLoop, calls=%fused_computation.45.clone.1 | loop fusion | flops 85970944 | bytes 122880 | tf_op jit(solution)/shard_map/while/body/eval_jaxpr/reduce_sum | solution.py:28
  160.6 16.2 %fusion.64 = (f32[2048]{0:T(1024)S(1)}, f32[2048]{0:T(1024)S(1)}, f32[2048]{0:T(1024)S(1)}, f32[2048]{0:T(1024)S(1)}, f32[2048]{0:T(1024)S(1)}, /*index=5*/f32[2048]{0:T(1024)S(1)}) fusion(f32[2048]{0:T(1024)S(1)} %bitcast.257, f32[1024]{0:T(1024)S(1)} %bitcast.269, f32[2048]{0:T(1024)S(1)} %bitcast.254, f32[1024]{0:T(1024)S(1)} %bitcast.272, ...), kind=kLoop, calls=%fused_computation.45.clone.1 | loop fusion | flops 85970944 | bytes 122880 | tf_op jit(solution)/shard_map/while/body/eval_jaxpr/reduce_sum | solution.py:28
  177.1 16.2 %fusion.64 = (f32[2048]{0:T(1024)S(1)}, f32[2048]{0:T(1024)S(1)}, f32[2048]{0:T(1024)S(1)}, f32[2048]{0:T(1024)S(1)}, f32[2048]{0:T(1024)S(1)}, /*index=5*/f32[2048]{0:T(1024)S(1)}) fusion(f32[2048]{0:T(1024)S(1)} %bitcast.257, f32[1024]{0:T(1024)S(1)} %bitcast.269, f32[2048]{0:T(1024)S(1)} %bitcast.254, f32[1024]{0:T(1024)S(1)} %bitcast.272, ...), kind=kLoop, calls=%fused_computation.45.clone.1 | loop fusion | flops 85970944 | bytes 122880 | tf_op jit(solution)/shard_map/while/body/eval_jaxpr/reduce_sum | solution.py:28
  193.5 16.2 %fusion.64 = (f32[2048]{0:T(1024)S(1)}, f32[2048]{0:T(1024)S(1)}, f32[2048]{0:T(1024)S(1)}, f32[2048]{0:T(1024)S(1)}, f32[2048]{0:T(1024)S(1)}, /*index=5*/f32[2048]{0:T(1024)S(1)}) fusion(f32[2048]{0:T(1024)S(1)} %bitcast.257, f32[1024]{0:T(1024)S(1)} %bitcast.269, f32[2048]{0:T(1024)S(1)} %bitcast.254, f32[1024]{0:T(1024)S(1)} %bitcast.272, ...), kind=kLoop, calls=%fused_computation.45.clone.1 | loop fusion | flops 85970944 | bytes 122880 | tf_op jit(solution)/shard_map/while/body/eval_jaxpr/reduce_sum | solution.py:28
  210.0 16.2 %fusion.64 = (f32[2048]{0:T(1024)S(1)}, f32[2048]{0:T(1024)S(1)}, f32[2048]{0:T(1024)S(1)}, f32[2048]{0:T(1024)S(1)}, f32[2048]{0:T(1024)S(1)}, /*index=5*/f32[2048]{0:T(1024)S(1)}) fusion(f32[2048]{0:T(1024)S(1)} %bitcast.257, f32[1024]{0:T(1024)S(1)} %bitcast.269, f32[2048]{0:T(1024)S(1)} %bitcast.254, f32[1024]{0:T(1024)S(1)} %bitcast.272, ...), kind=kLoop, calls=%fused_computation.45.clone.1 | loop fusion | flops 85970944 | bytes 122880 | tf_op jit(solution)/shard_map/while/body/eval_jaxpr/reduce_sum | solution.py:28
  226.4 16.2 %fusion.64 = (f32[2048]{0:T(1024)S(1)}, f32[2048]{0:T(1024)S(1)}, f32[2048]{0:T(1024)S(1)}, f32[2048]{0:T(1024)S(1)}, f32[2048]{0:T(1024)S(1)}, /*index=5*/f32[2048]{0:T(1024)S(1)}) fusion(f32[2048]{0:T(1024)S(1)} %bitcast.257, f32[1024]{0:T(1024)S(1)} %bitcast.269, f32[2048]{0:T(1024)S(1)} %bitcast.254, f32[1024]{0:T(1024)S(1)} %bitcast.272, ...), kind=kLoop, calls=%fused_computation.45.clone.1 | loop fusion | flops 85970944 | bytes 122880 | tf_op jit(solution)/shard_map/while/body/eval_jaxpr/reduce_sum | solution.py:28
  242.9 16.2 %fusion.64 = (f32[2048]{0:T(1024)S(1)}, f32[2048]{0:T(1024)S(1)}, f32[2048]{0:T(1024)S(1)}, f32[2048]{0:T(1024)S(1)}, f32[2048]{0:T(1024)S(1)}, /*index=5*/f32[2048]{0:T(1024)S(1)}) fusion(f32[2048]{0:T(1024)S(1)} %bitcast.257, f32[1024]{0:T(1024)S(1)} %bitcast.269, f32[2048]{0:T(1024)S(1)} %bitcast.254, f32[1024]{0:T(1024)S(1)} %bitcast.272, ...), kind=kLoop, calls=%fused_computation.45.clone.1 | loop fusion | flops 85970944 | bytes 122880 | tf_op jit(solution)/shard_map/while/body/eval_jaxpr/reduce_sum | solution.py:28
  259.3 16.2 %fusion.64 = (f32[2048]{0:T(1024)S(1)}, f32[2048]{0:T(1024)S(1)}, f32[2048]{0:T(1024)S(1)}, f32[2048]{0:T(1024)S(1)}, f32[2048]{0:T(1024)S(1)}, /*index=5*/f32[2048]{0:T(1024)S(1)}) fusion(f32[2048]{0:T(1024)S(1)} %bitcast.257, f32[1024]{0:T(1024)S(1)} %bitcast.269, f32[2048]{0:T(1024)S(1)} %bitcast.254, f32[1024]{0:T(1024)S(1)} %bitcast.272, ...), kind=kLoop, calls=%fused_computation.45.clone.1 | loop fusion | flops 85970944 | bytes 122880 | tf_op jit(solution)/shard_map/while/body/eval_jaxpr/reduce_sum | solution.py:28
  275.8 16.2 %fusion.64 = (f32[2048]{0:T(1024)S(1)}, f32[2048]{0:T(1024)S(1)}, f32[2048]{0:T(1024)S(1)}, f32[2048]{0:T(1024)S(1)}, f32[2048]{0:T(1024)S(1)}, /*index=5*/f32[2048]{0:T(1024)S(1)}) fusion(f32[2048]{0:T(1024)S(1)} %bitcast.257, f32[1024]{0:T(1024)S(1)} %bitcast.269, f32[2048]{0:T(1024)S(1)} %bitcast.254, f32[1024]{0:T(1024)S(1)} %bitcast.272, ...), kind=kLoop, calls=%fused_computation.45.clone.1 | loop fusion | flops 85970944 | bytes 122880 | tf_op jit(solution)/shard_map/while/body/eval_jaxpr/reduce_sum | solution.py:28
  292.2 16.2 %fusion.64 = (f32[2048]{0:T(1024)S(1)}, f32[2048]{0:T(1024)S(1)}, f32[2048]{0:T(1024)S(1)}, f32[2048]{0:T(1024)S(1)}, f32[2048]{0:T(1024)S(1)}, /*index=5*/f32[2048]{0:T(1024)S(1)}) fusion(f32[2048]{0:T(1024)S(1)} %bitcast.257, f32[1024]{0:T(1024)S(1)} %bitcast.269, f32[2048]{0:T(1024)S(1)} %bitcast.254, f32[1024]{0:T(1024)S(1)} %bitcast.272, ...), kind=kLoop, calls=%fused_computation.45.clone.1 | loop fusion | flops 85970944 | bytes 122880 | tf_op jit(solution)/shard_map/while/body/eval_jaxpr/reduce_sum | solution.py:28
  308.7 16.2 %fusion.64 = (f32[2048]{0:T(1024)S(1)}, f32[2048]{0:T(1024)S(1)}, f32[2048]{0:T(1024)S(1)}, f32[2048]{0:T(1024)S(1)}, f32[2048]{0:T(1024)S(1)}, /*index=5*/f32[2048]{0:T(1024)S(1)}) fusion(f32[2048]{0:T(1024)S(1)} %bitcast.257, f32[1024]{0:T(1024)S(1)} %bitcast.269, f32[2048]{0:T(1024)S(1)} %bitcast.254, f32[1024]{0:T(1024)S(1)} %bitcast.272, ...), kind=kLoop, calls=%fused_computation.45.clone.1 | loop fusion | flops 85970944 | bytes 122880 | tf_op jit(solution)/shard_map/while/body/eval_jaxpr/reduce_sum | solution.py:28
  325.1 16.2 %fusion.64 = (f32[2048]{0:T(1024)S(1)}, f32[2048]{0:T(1024)S(1)}, f32[2048]{0:T(1024)S(1)}, f32[2048]{0:T(1024)S(1)}, f32[2048]{0:T(1024)S(1)}, /*index=5*/f32[2048]{0:T(1024)S(1)}) fusion(f32[2048]{0:T(1024)S(1)} %bitcast.257, f32[1024]{0:T(1024)S(1)} %bitcast.269, f32[2048]{0:T(1024)S(1)} %bitcast.254, f32[1024]{0:T(1024)S(1)} %bitcast.272, ...), kind=kLoop, calls=%fused_computation.45.clone.1 | loop fusion | flops 85970944 | bytes 122880 | tf_op jit(solution)/shard_map/while/body/eval_jaxpr/reduce_sum | solution.py:28
  349.7 139.0 %all-reduce.3.cloned.1.call-done = f32[6,32768]{1,0:T(8,128)} async-done(((f32[6,32768]{1,0:T(8,128)}), f32[6,32768]{1,0:T(8,128)}) %all-reduce.3.cloned.1.call-update) | async-done | bytes 786448 | tf_op jit(solution)/shard_map/psum | solution.py:79
  498.1 64.6 %all-gather.3 = f32[128,6,256]{2,1,0:T(8,128)} all-gather(f32[1,6,256]{2,1,0:T(8,128)S(1)} %maximum_bitcast_fusion.1), channel_id=3, replica_groups=mesh['grp'=8,'dev'=16] {'grp','dev'}, dimensions={0}, use_global_device_ids=true | all-gather | bytes 792576 | tf_op jit(solution)/shard_map/all_gather | solution.py:76
  562.8 280.6 %while.21 = (s32[]{:T(128)}, f32[16,6,2048]{2,1,0:T(8,128)S(1)}, f32[3,1024]{1,0:T(4,128)S(1)}, f32[16,6,2048]{2,1,0:T(8,128)}, f32[3,1024]{1,0:T(4,128)S(1)}, /...) while((s32[]{:T(128)}, f32[16,6,2048]{2,1,0:T(8,128)S(1)}, ...), condition=%wide.region_21.22_spmd, body=%wide.region_14.21_spmd.sunk | while | flops 85970952 | bytes 499917 | solution.py:37
  564.0 16.2 %fusion.66 = (f32[2048]{0:T(1024)S(1)}, f32[2048]{0:T(1024)S(1)}, f32[2048]{0:T(1024)S(1)}, f32[2048]{0:T(1024)S(1)}, f32[2048]{0:T(1024)S(1)}, /*index=5*/f32[2048]{0:T(1024)S(1)}) fusion(f32[2048]{0:T(1024)S(1)} %bitcast.263, f32[1024]{0:T(1024)S(1)} %bitcast.275, f32[2048]{0:T(1024)S(1)} %bitcast.260, f32[1024]{0:T(1024)S(1)} %bitcast.278, ...), kind=kLoop, calls=%fused_computation.85.clone.1 | loop fusion | flops 85970944 | bytes 122880 | tf_op jit(solution)/shard_map/while/body/eval_jaxpr/reduce_sum | solution.py:28
  581.5 16.2 %fusion.66 = (f32[2048]{0:T(1024)S(1)}, f32[2048]{0:T(1024)S(1)}, f32[2048]{0:T(1024)S(1)}, f32[2048]{0:T(1024)S(1)}, f32[2048]{0:T(1024)S(1)}, /*index=5*/f32[2048]{0:T(1024)S(1)}) fusion(f32[2048]{0:T(1024)S(1)} %bitcast.263, f32[1024]{0:T(1024)S(1)} %bitcast.275, f32[2048]{0:T(1024)S(1)} %bitcast.260, f32[1024]{0:T(1024)S(1)} %bitcast.278, ...), kind=kLoop, calls=%fused_computation.85.clone.1 | loop fusion | flops 85970944 | bytes 122880 | tf_op jit(solution)/shard_map/while/body/eval_jaxpr/reduce_sum | solution.py:28
  599.2 16.2 %fusion.66 = (f32[2048]{0:T(1024)S(1)}, f32[2048]{0:T(1024)S(1)}, f32[2048]{0:T(1024)S(1)}, f32[2048]{0:T(1024)S(1)}, f32[2048]{0:T(1024)S(1)}, /*index=5*/f32[2048]{0:T(1024)S(1)}) fusion(f32[2048]{0:T(1024)S(1)} %bitcast.263, f32[1024]{0:T(1024)S(1)} %bitcast.275, f32[2048]{0:T(1024)S(1)} %bitcast.260, f32[1024]{0:T(1024)S(1)} %bitcast.278, ...), kind=kLoop, calls=%fused_computation.85.clone.1 | loop fusion | flops 85970944 | bytes 122880 | tf_op jit(solution)/shard_map/while/body/eval_jaxpr/reduce_sum | solution.py:28
  616.7 16.2 %fusion.66 = (f32[2048]{0:T(1024)S(1)}, f32[2048]{0:T(1024)S(1)}, f32[2048]{0:T(1024)S(1)}, f32[2048]{0:T(1024)S(1)}, f32[2048]{0:T(1024)S(1)}, /*index=5*/f32[2048]{0:T(1024)S(1)}) fusion(f32[2048]{0:T(1024)S(1)} %bitcast.263, f32[1024]{0:T(1024)S(1)} %bitcast.275, f32[2048]{0:T(1024)S(1)} %bitcast.260, f32[1024]{0:T(1024)S(1)} %bitcast.278, ...), kind=kLoop, calls=%fused_computation.85.clone.1 | loop fusion | flops 85970944 | bytes 122880 | tf_op jit(solution)/shard_map/while/body/eval_jaxpr/reduce_sum | solution.py:28
  634.2 16.2 %fusion.66 = (f32[2048]{0:T(1024)S(1)}, f32[2048]{0:T(1024)S(1)}, f32[2048]{0:T(1024)S(1)}, f32[2048]{0:T(1024)S(1)}, f32[2048]{0:T(1024)S(1)}, /*index=5*/f32[2048]{0:T(1024)S(1)}) fusion(f32[2048]{0:T(1024)S(1)} %bitcast.263, f32[1024]{0:T(1024)S(1)} %bitcast.275, f32[2048]{0:T(1024)S(1)} %bitcast.260, f32[1024]{0:T(1024)S(1)} %bitcast.278, ...), kind=kLoop, calls=%fused_computation.85.clone.1 | loop fusion | flops 85970944 | bytes 122880 | tf_op jit(solution)/shard_map/while/body/eval_jaxpr/reduce_sum | solution.py:28
  651.8 16.2 %fusion.66 = (f32[2048]{0:T(1024)S(1)}, f32[2048]{0:T(1024)S(1)}, f32[2048]{0:T(1024)S(1)}, f32[2048]{0:T(1024)S(1)}, f32[2048]{0:T(1024)S(1)}, /*index=5*/f32[2048]{0:T(1024)S(1)}) fusion(f32[2048]{0:T(1024)S(1)} %bitcast.263, f32[1024]{0:T(1024)S(1)} %bitcast.275, f32[2048]{0:T(1024)S(1)} %bitcast.260, f32[1024]{0:T(1024)S(1)} %bitcast.278, ...), kind=kLoop, calls=%fused_computation.85.clone.1 | loop fusion | flops 85970944 | bytes 122880 | tf_op jit(solution)/shard_map/while/body/eval_jaxpr/reduce_sum | solution.py:28
  669.3 16.2 %fusion.66 = (f32[2048]{0:T(1024)S(1)}, f32[2048]{0:T(1024)S(1)}, f32[2048]{0:T(1024)S(1)}, f32[2048]{0:T(1024)S(1)}, f32[2048]{0:T(1024)S(1)}, /*index=5*/f32[2048]{0:T(1024)S(1)}) fusion(f32[2048]{0:T(1024)S(1)} %bitcast.263, f32[1024]{0:T(1024)S(1)} %bitcast.275, f32[2048]{0:T(1024)S(1)} %bitcast.260, f32[1024]{0:T(1024)S(1)} %bitcast.278, ...), kind=kLoop, calls=%fused_computation.85.clone.1 | loop fusion | flops 85970944 | bytes 122880 | tf_op jit(solution)/shard_map/while/body/eval_jaxpr/reduce_sum | solution.py:28
  739.4 16.2 %fusion.66 = (f32[2048]{0:T(1024)S(1)}, f32[2048]{0:T(1024)S(1)}, f32[2048]{0:T(1024)S(1)}, f32[2048]{0:T(1024)S(1)}, f32[2048]{0:T(1024)S(1)}, /*index=5*/f32[2048]{0:T(1024)S(1)}) fusion(f32[2048]{0:T(1024)S(1)} %bitcast.263, f32[1024]{0:T(1024)S(1)} %bitcast.275, f32[2048]{0:T(1024)S(1)} %bitcast.260, f32[1024]{0:T(1024)S(1)} %bitcast.278, ...), kind=kLoop, calls=%fused_computation.85.clone.1 | loop fusion | flops 85970944 | bytes 122880 | tf_op jit(solution)/shard_map/while/body/eval_jaxpr/reduce_sum | solution.py:28
  757.0 16.2 %fusion.66 = (f32[2048]{0:T(1024)S(1)}, f32[2048]{0:T(1024)S(1)}, f32[2048]{0:T(1024)S(1)}, f32[2048]{0:T(1024)S(1)}, f32[2048]{0:T(1024)S(1)}, /*index=5*/f32[2048]{0:T(1024)S(1)}) fusion(f32[2048]{0:T(1024)S(1)} %bitcast.263, f32[1024]{0:T(1024)S(1)} %bitcast.275, f32[2048]{0:T(1024)S(1)} %bitcast.260, f32[1024]{0:T(1024)S(1)} %bitcast.278, ...), kind=kLoop, calls=%fused_computation.85.clone.1 | loop fusion | flops 85970944 | bytes 122880 | tf_op jit(solution)/shard_map/while/body/eval_jaxpr/reduce_sum | solution.py:28
  774.5 16.2 %fusion.66 = (f32[2048]{0:T(1024)S(1)}, f32[2048]{0:T(1024)S(1)}, f32[2048]{0:T(1024)S(1)}, f32[2048]{0:T(1024)S(1)}, f32[2048]{0:T(1024)S(1)}, /*index=5*/f32[2048]{0:T(1024)S(1)}) fusion(f32[2048]{0:T(1024)S(1)} %bitcast.263, f32[1024]{0:T(1024)S(1)} %bitcast.275, f32[2048]{0:T(1024)S(1)} %bitcast.260, f32[1024]{0:T(1024)S(1)} %bitcast.278, ...), kind=kLoop, calls=%fused_computation.85.clone.1 | loop fusion | flops 85970944 | bytes 122880 | tf_op jit(solution)/shard_map/while/body/eval_jaxpr/reduce_sum | solution.py:28
  849.1 141.9 %all-reduce.5.cloned.1.call-done = f32[6,32768]{1,0:T(8,128)} async-done(((f32[6,32768]{1,0:T(8,128)}), f32[6,32768]{1,0:T(8,128)}) %all-reduce.5.cloned.1.call-update) | async-done | bytes 786448 | tf_op jit(solution)/shard_map/psum | solution.py:79
  (223 shorter events, 160.9 us)
Async XLA Ops:
  7.2 481.4 %all-reduce.3.cloned.1.call-start = ((), (), s32[]{:S(2)}) async-start(), calls=%async_computation | async-start | bytes 2097152 | tf_op jit(solution)/shard_map/psum | solution.py:79
  341.5 1.0 copy-start.1
  341.5 1.1 copy-start.2
  341.5 1.3 copy-start.3
  341.5 1.6 copy-start.4
  342.5 0.8 copy-start.5
  342.6 648.4 %all-reduce.5.cloned.1.call-start = ((), (), s32[]{:S(2)}) async-start(), calls=%async_computation.1 | async-start | bytes 2097152 | tf_op jit(solution)/shard_map/psum | solution.py:79
  843.4 1.0 copy-start
Sparse Core Ops, SparseCore 0:
  342.7 145.8 all-reduce.2
  844.6 146.3 all-reduce.4
where the time goes:
time: 1010 us
  other arithmetic  525 us (52%)
  waiting for transfers between devices  281 us (28%)
  blocking collectives  129 us (13%)
  local copies, waits for them, and re-layouts  57.6 us (6%)
  between operations  14.4 us (1%)
    reduce_sum x32, other arithmetic, pair_block(): jnp.sum(weight * (drift_z - along * gap_z), axis=1)  519 us
    psum x2, waiting for transfers between devices, shards(): totals = lax.psum(terms, ('grp', 'dev'))  281 us
    all_gather x2, blocking collectives, shards(): gathered = lax.all_gather(targets[None], ('grp', 'dev'), axis=0, tiled=True)  129 us
  transfers between devices with their start and end apart: 2, of which 2 were waited for; matrix products, arithmetic and copies ran while one was open for 1% of the time, Pallas kernels for 0%

commit v1 on v0

--- a/solution.py
+++ b/solution.py
@@ -73,7 +73,12 @@
         targets = jnp.concatenate([pred_pos[:, rows], pred_vel[:, rows]], axis=0)
         step_counts = counts[step]
         own_count = step_counts[my_rank]
-        gathered = lax.all_gather(targets[None], ("grp", "dev"), axis=0, tiled=True)
+        gathered = jnp.concatenate(
+            lax.all_to_all(
+                jnp.stack([targets[None]] * lax.axis_size(("grp", "dev"))), ("grp", "dev"), 0, 0
+            ),
+            axis=0,
+        )
         flat = gathered.transpose(1, 0, 2).reshape(6, devices_all * slot_cap)
         terms = block_terms(flat, pred_pos, pred_vel, mass, soft_sq)
         totals = lax.psum(terms, ("grp", "dev"))

time: 1010 us -> 955 us (0.946)
  blocking collectives: 129 us -> 0 us
  local copies, waits for them, and re-layouts: 57.6 us -> 86.1 us
  waiting for transfers between devices: 281 us -> 307 us
  starting transfers between devices: 0.08 us -> 18.4 us
    all_gather x2 -> x0, blocking collectives: 129 us -> none  [shards(): gathered = lax.all_gather(targets[None], ('grp', 'dev'), axis=0, tiled=True)]
    all_to_all x0 -> x2, waiting for transfers between devices: none -> 24.6 us  [shards(): lax.all_to_all(jnp.stack([targets[None]] * lax.axis_size(('grp', 'dev')))...]
    all_to_all x0 -> x2, starting transfers between devices: none -> 18.3 us  [shards(): lax.all_to_all(jnp.stack([targets[None]] * lax.axis_size(('grp', 'dev')))...]
    slice x64, local copies, waits for them, and re-layouts: 20.1 us -> 37.6 us  [pair_block(): drift_x = src_vel[0][None, :] - targets[3][:, None]]
  transfers between devices with their start and end apart: 2 -> 4, of which waited for: 2 -> 4; matrix products, arithmetic and copies ran while one was open for 1% -> 1% of each run, Pallas kernels for 0% -> 0%
where the time goes in v1:
time: 955 us; the launch traced here: 952 us
  other arithmetic  525 us (55%)
  waiting for transfers between devices  307 us (32%)
  local copies, waits for them, and re-layouts  86.1 us (9%)
  starting transfers between devices  18.4 us (2%)
  between operations  14.4 us (2%)
    reduce_sum x32, other arithmetic, pair_block(): jnp.sum(weight * (drift_z - along * gap_z), axis=1)  519 us
    psum x2, waiting for transfers between devices, shards(): totals = lax.psum(terms, ('grp', 'dev'))  282 us
    slice x64, local copies, waits for them, and re-layouts, pair_block(): drift_x = src_vel[0][None, :] - targets[3][:, None]  37.6 us
    all_to_all x2, waiting for transfers between devices, shards(): lax.all_to_all(jnp.stack([targets[None]] * lax.axis_size(('grp', 'dev')))...  24.6 us
  transfers between devices with their start and end apart: 4, of which 4 were waited for; matrix products, arithmetic and copies ran while one was open for 1% of the time, Pallas kernels for 0%

profile of v1, /device:TPU:1, one launch (start us, length us, event | category | flops | bytes accessed | tf_op | source)
XLA Modules:
  0.0 952.1 jit_solution(11936273569696493552)
XLA Ops:
  47.3 280.6 %while.20 = (s32[]{:T(128)}, f32[16,6,2048]{2,1,0:T(8,128)S(1)}, f32[3,1024]{1,0:T(4,128)S(1)}, f32[16,6,2048]{2,1,0:T(8,128)}, f32[3,1024]{1,0:T(4,128)S(1)}, /...) while((s32[]{:T(128)}, f32[16,6,2048]{2,1,0:T(8,128)S(1)}, f32[3,1024]{1,0:T(4,128)S(1)}, ...), condition=%wide.region_7.8_spmd, body=%wide.region_0.7_spmd.sunk | while | flops 85970952 | bytes 499917 | solution.py:37
  48.5 16.2 %fusion.64 = (f32[2048]{0:T(1024)S(1)}, f32[2048]{0:T(1024)S(1)}, f32[2048]{0:T(1024)S(1)}, f32[2048]{0:T(1024)S(1)}, f32[2048]{0:T(1024)S(1)}, /*index=5*/f32[2048]{0:T(1024)S(1)}) fusion(f32[2048]{0:T(1024)S(1)} %bitcast.261, f32[1024]{0:T(1024)S(1)} %bitcast.273, f32[2048]{0:T(1024)S(1)} %bitcast.258, f32[1024]{0:T(1024)S(1)} %bitcast.276, ...), kind=kLoop, calls=%fused_computation.45.clone.1 | loop fusion | flops 85970944 | bytes 122880 | tf_op jit(solution)/shard_map/while/body/eval_jaxpr/reduce_sum | solution.py:28
  66.0 16.2 %fusion.64 = (f32[2048]{0:T(1024)S(1)}, f32[2048]{0:T(1024)S(1)}, f32[2048]{0:T(1024)S(1)}, f32[2048]{0:T(1024)S(1)}, f32[2048]{0:T(1024)S(1)}, /*index=5*/f32[2048]{0:T(1024)S(1)}) fusion(f32[2048]{0:T(1024)S(1)} %bitcast.261, f32[1024]{0:T(1024)S(1)} %bitcast.273, f32[2048]{0:T(1024)S(1)} %bitcast.258, f32[1024]{0:T(1024)S(1)} %bitcast.276, ...), kind=kLoop, calls=%fused_computation.45.clone.1 | loop fusion | flops 85970944 | bytes 122880 | tf_op jit(solution)/shard_map/while/body/eval_jaxpr/reduce_sum | solution.py:28
  83.7 16.2 %fusion.64 = (f32[2048]{0:T(1024)S(1)}, f32[2048]{0:T(1024)S(1)}, f32[2048]{0:T(1024)S(1)}, f32[2048]{0:T(1024)S(1)}, f32[2048]{0:T(1024)S(1)}, /*index=5*/f32[2048]{0:T(1024)S(1)}) fusion(f32[2048]{0:T(1024)S(1)} %bitcast.261, f32[1024]{0:T(1024)S(1)} %bitcast.273, f32[2048]{0:T(1024)S(1)} %bitcast.258, f32[1024]{0:T(1024)S(1)} %bitcast.276, ...), kind=kLoop, calls=%fused_computation.45.clone.1 | loop fusion | flops 85970944 | bytes 122880 | tf_op jit(solution)/shard_map/while/body/eval_jaxpr/reduce_sum | solution.py:28
  101.2 16.2 %fusion.64 = (f32[2048]{0:T(1024)S(1)}, f32[2048]{0:T(1024)S(1)}, f32[2048]{0:T(1024)S(1)}, f32[2048]{0:T(1024)S(1)}, f32[2048]{0:T(1024)S(1)}, /*index=5*/f32[2048]{0:T(1024)S(1)}) fusion(f32[2048]{0:T(1024)S(1)} %bitcast.261, f32[1024]{0:T(1024)S(1)} %bitcast.273, f32[2048]{0:T(1024)S(1)} %bitcast.258, f32[1024]{0:T(1024)S(1)} %bitcast.276, ...), kind=kLoop, calls=%fused_computation.45.clone.1 | loop fusion | flops 85970944 | bytes 122880 | tf_op jit(solution)/shard_map/while/body/eval_jaxpr/reduce_sum | solution.py:28
  136.3 16.2 %fusion.64 = (f32[2048]{0:T(1024)S(1)}, f32[2048]{0:T(1024)S(1)}, f32[2048]{0:T(1024)S(1)}, f32[2048]{0:T(1024)S(1)}, f32[2048]{0:T(1024)S(1)}, /*index=5*/f32[2048]{0:T(1024)S(1)}) fusion(f32[2048]{0:T(1024)S(1)} %bitcast.261, f32[1024]{0:T(1024)S(1)} %bitcast.273, f32[2048]{0:T(1024)S(1)} %bitcast.258, f32[1024]{0:T(1024)S(1)} %bitcast.276, ...), kind=kLoop, calls=%fused_computation.45.clone.1 | loop fusion | flops 85970944 | bytes 122880 | tf_op jit(solution)/shard_map/while/body/eval_jaxpr/reduce_sum | solution.py:28
  171.4 16.2 %fusion.64 = (f32[2048]{0:T(1024)S(1)}, f32[2048]{0:T(1024)S(1)}, f32[2048]{0:T(1024)S(1)}, f32[2048]{0:T(1024)S(1)}, f32[2048]{0:T(1024)S(1)}, /*index=5*/f32[2048]{0:T(1024)S(1)}) fusion(f32[2048]{0:T(1024)S(1)} %bitcast.261, f32[1024]{0:T(1024)S(1)} %bitcast.273, f32[2048]{0:T(1024)S(1)} %bitcast.258, f32[1024]{0:T(1024)S(1)} %bitcast.276, ...), kind=kLoop, calls=%fused_computation.45.clone.1 | loop fusion | flops 85970944 | bytes 122880 | tf_op jit(solution)/shard_map/while/body/eval_jaxpr/reduce_sum | solution.py:28
  188.9 16.2 %fusion.64 = (f32[2048]{0:T(1024)S(1)}, f32[2048]{0:T(1024)S(1)}, f32[2048]{0:T(1024)S(1)}, f32[2048]{0:T(1024)S(1)}, f32[2048]{0:T(1024)S(1)}, /*index=5*/f32[2048]{0:T(1024)S(1)}) fusion(f32[2048]{0:T(1024)S(1)} %bitcast.261, f32[1024]{0:T(1024)S(1)} %bitcast.273, f32[2048]{0:T(1024)S(1)} %bitcast.258, f32[1024]{0:T(1024)S(1)} %bitcast.276, ...), kind=kLoop, calls=%fused_computation.45.clone.1 | loop fusion | flops 85970944 | bytes 122880 | tf_op jit(solution)/shard_map/while/body/eval_jaxpr/reduce_sum | solution.py:28
  206.4 16.2 %fusion.64 = (f32[2048]{0:T(1024)S(1)}, f32[2048]{0:T(1024)S(1)}, f32[2048]{0:T(1024)S(1)}, f32[2048]{0:T(1024)S(1)}, f32[2048]{0:T(1024)S(1)}, /*index=5*/f32[2048]{0:T(1024)S(1)}) fusion(f32[2048]{0:T(1024)S(1)} %bitcast.261, f32[1024]{0:T(1024)S(1)} %bitcast.273, f32[2048]{0:T(1024)S(1)} %bitcast.258, f32[1024]{0:T(1024)S(1)} %bitcast.276, ...), kind=kLoop, calls=%fused_computation.45.clone.1 | loop fusion | flops 85970944 | bytes 122880 | tf_op jit(solution)/shard_map/while/body/eval_jaxpr/reduce_sum | solution.py:28
  259.0 16.2 %fusion.64 = (f32[2048]{0:T(1024)S(1)}, f32[2048]{0:T(1024)S(1)}, f32[2048]{0:T(1024)S(1)}, f32[2048]{0:T(1024)S(1)}, f32[2048]{0:T(1024)S(1)}, /*index=5*/f32[2048]{0:T(1024)S(1)}) fusion(f32[2048]{0:T(1024)S(1)} %bitcast.261, f32[1024]{0:T(1024)S(1)} %bitcast.273, f32[2048]{0:T(1024)S(1)} %bitcast.258, f32[1024]{0:T(1024)S(1)} %bitcast.276, ...), kind=kLoop, calls=%fused_computation.45.clone.1 | loop fusion | flops 85970944 | bytes 122880 | tf_op jit(solution)/shard_map/while/body/eval_jaxpr/reduce_sum | solution.py:28
  276.5 16.2 %fusion.64 = (f32[2048]{0:T(1024)S(1)}, f32[2048]{0:T(1024)S(1)}, f32[2048]{0:T(1024)S(1)}, f32[2048]{0:T(1024)S(1)}, f32[2048]{0:T(1024)S(1)}, /*index=5*/f32[2048]{0:T(1024)S(1)}) fusion(f32[2048]{0:T(1024)S(1)} %bitcast.261, f32[1024]{0:T(1024)S(1)} %bitcast.273, f32[2048]{0:T(1024)S(1)} %bitcast.258, f32[1024]{0:T(1024)S(1)} %bitcast.276, ...), kind=kLoop, calls=%fused_computation.45.clone.1 | loop fusion | flops 85970944 | bytes 122880 | tf_op jit(solution)/shard_map/while/body/eval_jaxpr/reduce_sum | solution.py:28
  294.1 16.2 %fusion.64 = (f32[2048]{0:T(1024)S(1)}, f32[2048]{0:T(1024)S(1)}, f32[2048]{0:T(1024)S(1)}, f32[2048]{0:T(1024)S(1)}, f32[2048]{0:T(1024)S(1)}, /*index=5*/f32[2048]{0:T(1024)S(1)}) fusion(f32[2048]{0:T(1024)S(1)} %bitcast.261, f32[1024]{0:T(1024)S(1)} %bitcast.273, f32[2048]{0:T(1024)S(1)} %bitcast.258, f32[1024]{0:T(1024)S(1)} %bitcast.276, ...), kind=kLoop, calls=%fused_computation.45.clone.1 | loop fusion | flops 85970944 | bytes 122880 | tf_op jit(solution)/shard_map/while/body/eval_jaxpr/reduce_sum | solution.py:28
  311.6 16.2 %fusion.64 = (f32[2048]{0:T(1024)S(1)}, f32[2048]{0:T(1024)S(1)}, f32[2048]{0:T(1024)S(1)}, f32[2048]{0:T(1024)S(1)}, f32[2048]{0:T(1024)S(1)}, /*index=5*/f32[2048]{0:T(1024)S(1)}) fusion(f32[2048]{0:T(1024)S(1)} %bitcast.261, f32[1024]{0:T(1024)S(1)} %bitcast.273, f32[2048]{0:T(1024)S(1)} %bitcast.258, f32[1024]{0:T(1024)S(1)} %bitcast.276, ...), kind=kLoop, calls=%fused_computation.45.clone.1 | loop fusion | flops 85970944 | bytes 122880 | tf_op jit(solution)/shard_map/while/body/eval_jaxpr/reduce_sum | solution.py:28
  329.0 143.4 %all-reduce.3.cloned.1.call-done = f32[6,32768]{1,0:T(8,128)} async-done(((f32[6,32768]{1,0:T(8,128)}), f32[6,32768]{1,0:T(8,128)}) %all-reduce.3.cloned.1.call-update) | async-done | bytes 786448 | tf_op jit(solution)/shard_map/psum | solution.py:84
  510.0 280.8 %while.21 = (s32[]{:T(128)}, f32[16,6,2048]{2,1,0:T(8,128)S(1)}, f32[3,1024]{1,0:T(4,128)S(1)}, f32[16,6,2048]{2,1,0:T(8,128)}, f32[3,1024]{1,0:T(4,128)S(1)}, /...) while((s32[]{:T(128)}, f32[16,6,2048]{2,1,0:T(8,128)S(1)}, ...), condition=%wide.region_21.22_spmd, body=%wide.region_14.21_spmd.sunk | while | flops 85970952 | bytes 499917 | solution.py:37
  511.2 16.2 %fusion.66 = (f32[2048]{0:T(1024)S(1)}, f32[2048]{0:T(1024)S(1)}, f32[2048]{0:T(1024)S(1)}, f32[2048]{0:T(1024)S(1)}, f32[2048]{0:T(1024)S(1)}, /*index=5*/f32[2048]{0:T(1024)S(1)}) fusion(f32[2048]{0:T(1024)S(1)} %bitcast.267, f32[1024]{0:T(1024)S(1)} %bitcast.279, f32[2048]{0:T(1024)S(1)} %bitcast.264, f32[1024]{0:T(1024)S(1)} %bitcast.282, ...), kind=kLoop, calls=%fused_computation.85.clone.1 | loop fusion | flops 85970944 | bytes 122880 | tf_op jit(solution)/shard_map/while/body/eval_jaxpr/reduce_sum | solution.py:28
  528.7 16.2 %fusion.66 = (f32[2048]{0:T(1024)S(1)}, f32[2048]{0:T(1024)S(1)}, f32[2048]{0:T(1024)S(1)}, f32[2048]{0:T(1024)S(1)}, f32[2048]{0:T(1024)S(1)}, /*index=5*/f32[2048]{0:T(1024)S(1)}) fusion(f32[2048]{0:T(1024)S(1)} %bitcast.267, f32[1024]{0:T(1024)S(1)} %bitcast.279, f32[2048]{0:T(1024)S(1)} %bitcast.264, f32[1024]{0:T(1024)S(1)} %bitcast.282, ...), kind=kLoop, calls=%fused_computation.85.clone.1 | loop fusion | flops 85970944 | bytes 122880 | tf_op jit(solution)/shard_map/while/body/eval_jaxpr/reduce_sum | solution.py:28
  546.4 16.2 %fusion.66 = (f32[2048]{0:T(1024)S(1)}, f32[2048]{0:T(1024)S(1)}, f32[2048]{0:T(1024)S(1)}, f32[2048]{0:T(1024)S(1)}, f32[2048]{0:T(1024)S(1)}, /*index=5*/f32[2048]{0:T(1024)S(1)}) fusion(f32[2048]{0:T(1024)S(1)} %bitcast.267, f32[1024]{0:T(1024)S(1)} %bitcast.279, f32[2048]{0:T(1024)S(1)} %bitcast.264, f32[1024]{0:T(1024)S(1)} %bitcast.282, ...), kind=kLoop, calls=%fused_computation.85.clone.1 | loop fusion | flops 85970944 | bytes 122880 | tf_op jit(solution)/shard_map/while/body/eval_jaxpr/reduce_sum | solution.py:28
  563.9 16.2 %fusion.66 = (f32[2048]{0:T(1024)S(1)}, f32[2048]{0:T(1024)S(1)}, f32[2048]{0:T(1024)S(1)}, f32[2048]{0:T(1024)S(1)}, f32[2048]{0:T(1024)S(1)}, /*index=5*/f32[2048]{0:T(1024)S(1)}) fusion(f32[2048]{0:T(1024)S(1)} %bitcast.267, f32[1024]{0:T(1024)S(1)} %bitcast.279, f32[2048]{0:T(1024)S(1)} %bitcast.264, f32[1024]{0:T(1024)S(1)} %bitcast.282, ...), kind=kLoop, calls=%fused_computation.85.clone.1 | loop fusion | flops 85970944 | bytes 122880 | tf_op jit(solution)/shard_map/while/body/eval_jaxpr/reduce_sum | solution.py:28
  581.4 16.2 %fusion.66 = (f32[2048]{0:T(1024)S(1)}, f32[2048]{0:T(1024)S(1)}, f32[2048]{0:T(1024)S(1)}, f32[2048]{0:T(1024)S(1)}, f32[2048]{0:T(1024)S(1)}, /*index=5*/f32[2048]{0:T(1024)S(1)}) fusion(f32[2048]{0:T(1024)S(1)} %bitcast.267, f32[1024]{0:T(1024)S(1)} %bitcast.279, f32[2048]{0:T(1024)S(1)} %bitcast.264, f32[1024]{0:T(1024)S(1)} %bitcast.282, ...), kind=kLoop, calls=%fused_computation.85.clone.1 | loop fusion | flops 85970944 | bytes 122880 | tf_op jit(solution)/shard_map/while/body/eval_jaxpr/reduce_sum | solution.py:28
  599.0 16.2 %fusion.66 = (f32[2048]{0:T(1024)S(1)}, f32[2048]{0:T(1024)S(1)}, f32[2048]{0:T(1024)S(1)}, f32[2048]{0:T(1024)S(1)}, f32[2048]{0:T(1024)S(1)}, /*index=5*/f32[2048]{0:T(1024)S(1)}) fusion(f32[2048]{0:T(1024)S(1)} %bitcast.267, f32[1024]{0:T(1024)S(1)} %bitcast.279, f32[2048]{0:T(1024)S(1)} %bitcast.264, f32[1024]{0:T(1024)S(1)} %bitcast.282, ...), kind=kLoop, calls=%fused_computation.85.clone.1 | loop fusion | flops 85970944 | bytes 122880 | tf_op jit(solution)/shard_map/while/body/eval_jaxpr/reduce_sum | solution.py:28
  616.5 16.2 %fusion.66 = (f32[2048]{0:T(1024)S(1)}, f32[2048]{0:T(1024)S(1)}, f32[2048]{0:T(1024)S(1)}, f32[2048]{0:T(1024)S(1)}, f32[2048]{0:T(1024)S(1)}, /*index=5*/f32[2048]{0:T(1024)S(1)}) fusion(f32[2048]{0:T(1024)S(1)} %bitcast.267, f32[1024]{0:T(1024)S(1)} %bitcast.279, f32[2048]{0:T(1024)S(1)} %bitcast.264, f32[1024]{0:T(1024)S(1)} %bitcast.282, ...), kind=kLoop, calls=%fused_computation.85.clone.1 | loop fusion | flops 85970944 | bytes 122880 | tf_op jit(solution)/shard_map/while/body/eval_jaxpr/reduce_sum | solution.py:28
  634.1 16.2 %fusion.66 = (f32[2048]{0:T(1024)S(1)}, f32[2048]{0:T(1024)S(1)}, f32[2048]{0:T(1024)S(1)}, f32[2048]{0:T(1024)S(1)}, f32[2048]{0:T(1024)S(1)}, /*index=5*/f32[2048]{0:T(1024)S(1)}) fusion(f32[2048]{0:T(1024)S(1)} %bitcast.267, f32[1024]{0:T(1024)S(1)} %bitcast.279, f32[2048]{0:T(1024)S(1)} %bitcast.264, f32[1024]{0:T(1024)S(1)} %bitcast.282, ...), kind=kLoop, calls=%fused_computation.85.clone.1 | loop fusion | flops 85970944 | bytes 122880 | tf_op jit(solution)/shard_map/while/body/eval_jaxpr/reduce_sum | solution.py:28
  651.6 16.2 %fusion.66 = (f32[2048]{0:T(1024)S(1)}, f32[2048]{0:T(1024)S(1)}, f32[2048]{0:T(1024)S(1)}, f32[2048]{0:T(1024)S(1)}, f32[2048]{0:T(1024)S(1)}, /*index=5*/f32[2048]{0:T(1024)S(1)}) fusion(f32[2048]{0:T(1024)S(1)} %bitcast.267, f32[1024]{0:T(1024)S(1)} %bitcast.279, f32[2048]{0:T(1024)S(1)} %bitcast.264, f32[1024]{0:T(1024)S(1)} %bitcast.282, ...), kind=kLoop, calls=%fused_computation.85.clone.1 | loop fusion | flops 85970944 | bytes 122880 | tf_op jit(solution)/shard_map/while/body/eval_jaxpr/reduce_sum | solution.py:28
  669.1 16.2 %fusion.66 = (f32[2048]{0:T(1024)S(1)}, f32[2048]{0:T(1024)S(1)}, f32[2048]{0:T(1024)S(1)}, f32[2048]{0:T(1024)S(1)}, f32[2048]{0:T(1024)S(1)}, /*index=5*/f32[2048]{0:T(1024)S(1)}) fusion(f32[2048]{0:T(1024)S(1)} %bitcast.267, f32[1024]{0:T(1024)S(1)} %bitcast.279, f32[2048]{0:T(1024)S(1)} %bitcast.264, f32[1024]{0:T(1024)S(1)} %bitcast.282, ...), kind=kLoop, calls=%fused_computation.85.clone.1 | loop fusion | flops 85970944 | bytes 122880 | tf_op jit(solution)/shard_map/while/body/eval_jaxpr/reduce_sum | solution.py:28
  686.7 16.2 %fusion.66 = (f32[2048]{0:T(1024)S(1)}, f32[2048]{0:T(1024)S(1)}, f32[2048]{0:T(1024)S(1)}, f32[2048]{0:T(1024)S(1)}, f32[2048]{0:T(1024)S(1)}, /*index=5*/f32[2048]{0:T(1024)S(1)}) fusion(f32[2048]{0:T(1024)S(1)} %bitcast.267, f32[1024]{0:T(1024)S(1)} %bitcast.279, f32[2048]{0:T(1024)S(1)} %bitcast.264, f32[1024]{0:T(1024)S(1)} %bitcast.282, ...), kind=kLoop, calls=%fused_computation.85.clone.1 | loop fusion | flops 85970944 | bytes 122880 | tf_op jit(solution)/shard_map/while/body/eval_jaxpr/reduce_sum | solution.py:28
  704.2 16.2 %fusion.66 = (f32[2048]{0:T(1024)S(1)}, f32[2048]{0:T(1024)S(1)}, f32[2048]{0:T(1024)S(1)}, f32[2048]{0:T(1024)S(1)}, f32[2048]{0:T(1024)S(1)}, /*index=5*/f32[2048]{0:T(1024)S(1)}) fusion(f32[2048]{0:T(1024)S(1)} %bitcast.267, f32[1024]{0:T(1024)S(1)} %bitcast.279, f32[2048]{0:T(1024)S(1)} %bitcast.264, f32[1024]{0:T(1024)S(1)} %bitcast.282, ...), kind=kLoop, calls=%fused_computation.85.clone.1 | loop fusion | flops 85970944 | bytes 122880 | tf_op jit(solution)/shard_map/while/body/eval_jaxpr/reduce_sum | solution.py:28
  721.8 16.2 %fusion.66 = (f32[2048]{0:T(1024)S(1)}, f32[2048]{0:T(1024)S(1)}, f32[2048]{0:T(1024)S(1)}, f32[2048]{0:T(1024)S(1)}, f32[2048]{0:T(1024)S(1)}, /*index=5*/f32[2048]{0:T(1024)S(1)}) fusion(f32[2048]{0:T(1024)S(1)} %bitcast.267, f32[1024]{0:T(1024)S(1)} %bitcast.279, f32[2048]{0:T(1024)S(1)} %bitcast.264, f32[1024]{0:T(1024)S(1)} %bitcast.282, ...), kind=kLoop, calls=%fused_computation.85.clone.1 | loop fusion | flops 85970944 | bytes 122880 | tf_op jit(solution)/shard_map/while/body/eval_jaxpr/reduce_sum | solution.py:28
  739.3 16.2 %fusion.66 = (f32[2048]{0:T(1024)S(1)}, f32[2048]{0:T(1024)S(1)}, f32[2048]{0:T(1024)S(1)}, f32[2048]{0:T(1024)S(1)}, f32[2048]{0:T(1024)S(1)}, /*index=5*/f32[2048]{0:T(1024)S(1)}) fusion(f32[2048]{0:T(1024)S(1)} %bitcast.267, f32[1024]{0:T(1024)S(1)} %bitcast.279, f32[2048]{0:T(1024)S(1)} %bitcast.264, f32[1024]{0:T(1024)S(1)} %bitcast.282, ...), kind=kLoop, calls=%fused_computation.85.clone.1 | loop fusion | flops 85970944 | bytes 122880 | tf_op jit(solution)/shard_map/while/body/eval_jaxpr/reduce_sum | solution.py:28
  756.8 16.2 %fusion.66 = (f32[2048]{0:T(1024)S(1)}, f32[2048]{0:T(1024)S(1)}, f32[2048]{0:T(1024)S(1)}, f32[2048]{0:T(1024)S(1)}, f32[2048]{0:T(1024)S(1)}, /*index=5*/f32[2048]{0:T(1024)S(1)}) fusion(f32[2048]{0:T(1024)S(1)} %bitcast.267, f32[1024]{0:T(1024)S(1)} %bitcast.279, f32[2048]{0:T(1024)S(1)} %bitcast.264, f32[1024]{0:T(1024)S(1)} %bitcast.282, ...), kind=kLoop, calls=%fused_computation.85.clone.1 | loop fusion | flops 85970944 | bytes 122880 | tf_op jit(solution)/shard_map/while/body/eval_jaxpr/reduce_sum | solution.py:28
  774.4 16.2 %fusion.66 = (f32[2048]{0:T(1024)S(1)}, f32[2048]{0:T(1024)S(1)}, f32[2048]{0:T(1024)S(1)}, f32[2048]{0:T(1024)S(1)}, f32[2048]{0:T(1024)S(1)}, /*index=5*/f32[2048]{0:T(1024)S(1)}) fusion(f32[2048]{0:T(1024)S(1)} %bitcast.267, f32[1024]{0:T(1024)S(1)} %bitcast.279, f32[2048]{0:T(1024)S(1)} %bitcast.264, f32[1024]{0:T(1024)S(1)} %bitcast.282, ...), kind=kLoop, calls=%fused_computation.85.clone.1 | loop fusion | flops 85970944 | bytes 122880 | tf_op jit(solution)/shard_map/while/body/eval_jaxpr/reduce_sum | solution.py:28
  796.4 138.7 %all-reduce.5.cloned.1.call-done = f32[6,32768]{1,0:T(8,128)} async-done(((f32[6,32768]{1,0:T(8,128)}), f32[6,32768]{1,0:T(8,128)}) %all-reduce.5.cloned.1.call-update) | async-done | bytes 786448 | tf_op jit(solution)/shard_map/psum | solution.py:84
  (235 shorter events, 199.8 us)
Async XLA Ops:
  14.2 12.9 %copy-start.3 = (f32[3,1024]{1,0:T(4,128)S(1)}, f32[3,1024]{1,0:T(4,128)}, u32[]{:S(2)}) copy-start(f32[3,1024]{1,0:T(4,128)} %param.11) | copy-start | bytes 36868
  15.5 11.8 %copy-start.4 = (f32[3,1024]{1,0:T(4,128)S(1)}, f32[3,1024]{1,0:T(4,128)}, u32[]{:S(2)}) copy-start(f32[3,1024]{1,0:T(4,128)} %param.12) | copy-start | bytes 36868
  15.5 12.0 %copy-start.5 = (f32[3,1024]{1,0:T(4,128)S(1)}, f32[3,1024]{1,0:T(4,128)}, u32[]{:S(2)}) copy-start(f32[3,1024]{1,0:T(4,128)} %param.13) | copy-start | bytes 36868
  15.5 28.1 %all-to-all-start = ((f32[128,1,6,256]{3,1,2,0:T(1,128)}), f32[128,1,6,256]{3,1,2,0:T(1,128)S(1)}, u32[]{:S(2)}, u32[]{:S(2)}) async-start(f32[128,1,6,256]{3,1,2,0:T(1,128)} %stack.48), calls=%async_computation | async-start | bytes 1572864 | tf_op jit(solution)/shard_map/all_to_all | solution.py:77
  27.0 0.8 copy-start.6
  27.0 445.4 %all-reduce.3.cloned.1.call-start = ((), (), s32[]{:S(2)}) async-start(), calls=%async_computation.2 | async-start | bytes 2097152 | tf_op jit(solution)/shard_map/psum | solution.py:84
  327.9 1.0 copy-start.1
  479.9 2.9 copy-start.2
  482.8 23.4 %all-to-all-start.1 = ((f32[128,1,6,256]{3,1,2,0:T(1,128)}), f32[128,1,6,256]{3,1,2,0:T(1,128)S(1)}, u32[]{:S(2)}, u32[]{:S(2)}) async-start(f32[128,1,6,256]{3,1,2,0:T(1,128)} %stack.49), calls=%async_computation.1 | async-start | bytes 1572864 | tf_op jit(solution)/shard_map/all_to_all | solution.py:77
  489.6 445.6 %all-reduce.5.cloned.1.call-start = ((), (), s32[]{:S(2)}) async-start(), calls=%async_computation.3 | async-start | bytes 2097152 | tf_op jit(solution)/shard_map/psum | solution.py:84
  790.7 1.0 copy-start
Sparse Core Ops, SparseCore 0:
  329.1 143.2 all-reduce.2
  791.9 143.2 all-reduce.4
